TPU v7x, 256 devices: a whole 4x4x8 slice. The times are simulated.
256 devices in a mesh: obs: 64 (over y, x, z_lo), ens: 4 (over z_hi, core).
Axes of the slice: x: 4, y: 4, z: 8 (z_hi: 2, z_lo: 4; z = z_hi * 4 + z_lo), core: 2. Of those that a mesh axis runs over, the one named last changes fastest.
Arguments:
- predicted: bfloat16 [262144, 512], P('obs', 'ens'), as said below
- noise: bfloat16 [262144, 512], P('obs', 'ens'), may hold values from -5 to 5
- observed: float32 [262144], P('obs'), as said below
- obs_error: float32 [262144], P('obs'), as said below
- coefficients: float32 [2000, 512], P('ens'), may hold values from -6 to 6
- basis: bfloat16 [2000, 262144], P(None, ('obs', 'ens')), may hold values from -0.125 to 0.125
- mean_field: float32 [262144], P(('obs', 'ens')), may hold values from -5 to 5
Outputs:
- updated: float32 [2000, 512], P('ens')
- field: bfloat16 [512, 262144], P(None, ('obs', 'ens'))
Inputs may be any that keep to these rules, and one draw needn't show every extreme that they name: `observed`: observed data of order sqrt(512). `obs_error`: error deviations between half and twice sqrt(512). `predicted`: predicted data of order one.
All inputs are finite; a program needn't handle non-finite values.
Results may differ from a plain program's by a relative error of at most 0.0095.
Values may be sent and summed in bfloat16 or wider, within the bound.
No kernel may reach another device: no remote copies, remote signals or barrier semaphores. Data moves between devices by JAX's collectives and lax.ppermute only.
A program may use at most 64 MiB of HBM per device.

v0:
```python
import jax
import jax.numpy as jnp
from jax import lax
from jax.sharding import PartitionSpec as P

ALPHA = 4


def member_products(gathered, innov_all, row_scale, members):
    pred_wide = gathered.astype(jnp.float32)
    row_mean = jnp.mean(pred_wide, axis=1, keepdims=True)
    anomaly = ((pred_wide - row_mean) / ((members - 1) ** 0.5 * row_scale[:, None])).astype(
        jnp.bfloat16
    )
    contract = (((0,), (0,)), ((), ()))
    gram_part = lax.dot_general(anomaly, anomaly, contract, preferred_element_type=jnp.float32)
    cross_part = lax.dot_general(anomaly, innov_all, contract, preferred_element_type=jnp.float32)
    return (gram_part, cross_part)


def shards(predicted, noise, observed, obs_error, coefficients, basis, mean_field):
    row_count, group_size = predicted.shape
    members = group_size * lax.axis_size("ens")
    spread = ALPHA**0.5 * obs_error
    innovation = (
        (observed[:, None] - predicted.astype(jnp.float32)) / spread[:, None]
        + noise.astype(jnp.float32)
    ).astype(jnp.bfloat16)
    gathered, innov_all = (
        lax.all_gather(predicted, "ens", axis=1, tiled=True),
        lax.all_gather(innovation, "ens", axis=1, tiled=True),
    )
    gram_part, cross_part = member_products(gathered, innov_all, spread, members)
    gram_sum, cross = lax.psum((gram_part, cross_part), "obs")
    gram = gram_sum + jnp.eye(members, dtype=jnp.float32)
    factor = jnp.linalg.cholesky(gram)
    weights = jax.scipy.linalg.cho_solve((factor, True), cross)
    coef_mean = jnp.mean(coefficients, axis=1, keepdims=True)
    coef_anomaly = (coefficients - coef_mean) / (members - 1) ** 0.5
    updated = coefficients + jnp.dot(coef_anomaly, weights, precision=lax.Precision.HIGHEST)
    coef_low = updated.astype(jnp.bfloat16)
    rebuilt = lax.dot_general(
        lax.all_gather(coef_low, "ens", axis=0, tiled=True),
        basis,
        (((0,), (0,)), ((), ())),
        preferred_element_type=jnp.float32,
    )
    field = (mean_field[None, :] + rebuilt).astype(jnp.bfloat16)
    return (updated, field)


def solution(mesh):
    in_specs = (
        P("obs", "ens"),
        P("obs", "ens"),
        P("obs"),
        P("obs"),
        P("ens", None),
        P(None, ("obs", "ens")),
        P(("obs", "ens")),
    )
    out_specs = (P("ens", None), P(None, ("obs", "ens")))
    return jax.shard_map(shards, mesh=mesh, in_specs=in_specs, out_specs=out_specs, check_vma=False)
```

profile of v0, /device:TPU:1, one launch (start us, length us, event | category | flops | bytes accessed | tf_op | source)
XLA Modules:
  0.0 1074.3 jit_solution(3603929709403278872)
XLA Ops:
  7.2 0.7 all-gather.5.cloned.1.call-update
  7.9 0.7 broadcast_multiply_fusion
  8.7 5.5 add_convert_fusion.1
  14.2 66.9 %all-gather.5.cloned.1.call-done = bf16[4096,512]{1,0:T(8,128)(2,1)} async-done(((bf16[4096,128]{1,0:T(8,128)(2,1)}), bf16[4096,512]{1,0:T(8,128)(2,1)}) %all-gather.5.cloned.1.call-update) | async-done | bytes 4194320 | tf_op jit(solution)/shard_map/all_gather | solution.py:30
  81.1 3.0 convert_reduce_fusion
  84.1 0.5 copy-done.1
  84.5 2.8 fusion.1
  87.3 2.0 copy-done
  89.3 3.4 fusion.63
  92.7 53.9 %all-gather.7.cloned.1.call-done = bf16[4096,512]{1,0:T(8,128)(2,1)} async-done(((bf16[4096,128]{1,0:T(8,128)(2,1)}), bf16[4096,512]{1,0:T(8,128)(2,1)}) %all-gather.7.cloned.1.call-update) | async-done | bytes 4194320 | tf_op jit(solution)/shard_map/all_gather | solution.py:31
  146.7 6.8 fusion.64
  153.5 0.5 all-gather.9.cloned.1.call-start
  154.2 671.9 %all-reduce.4.cloned.1.call-done = (f32[512,512]{1,0:T(8,128)}, f32[512,512]{0,1:T(8,128)}) async-done(((f32[512,512]{1,0:T(8,128)}, f32[512,512]{0,1:T(8,128)}), (f32[512,512]{1,0:T(8,128)}, f32[512,512]{0,1:T(8,128)})) %all-reduce.4.cloned.1.call-update) | async-done | bytes 2097168 | tf_op jit(solution)/shard_map/psum | solution.py:34
  826.1 1.4 convert_add_fusion
  828.1 11.7 %cholesky.104 = f32[128,128]{1,0:T(8,128)S(1)} custom-call(f32[128,128]{1,0:T(8,128)S(1)} %cholesky.266), custom_call_target="Cholesky" | custom-call | tf_op jit(solution)/shard_map/jit(cholesky)/cholesky | solution.py:36
  840.0 9.8 custom-call.34
  850.5 11.7 %cholesky.217 = f32[128,128]{1,0:T(8,128)S(1)} custom-call(f32[128,128]{1,0:T(8,128)S(1)} %cholesky.270), custom_call_target="Cholesky" | custom-call | tf_op jit(solution)/shard_map/jit(cholesky)/cholesky | solution.py:36
  862.2 10.0 custom-call.35
  872.8 11.7 %cholesky.238 = f32[128,128]{1,0:T(8,128)S(1)} custom-call(f32[128,128]{1,0:T(8,128)S(1)} %cholesky.275), custom_call_target="Cholesky" | custom-call | tf_op jit(solution)/shard_map/jit(cholesky)/cholesky | solution.py:36
  884.6 0.7 compare_reduce_fusion.1
  885.3 9.8 custom-call.36
  895.7 11.7 %cholesky.255 = f32[128,128]{1,0:T(8,128)S(1)} custom-call(f32[128,128]{1,0:T(8,128)S(1)} %convolution_subtract_fusion.8), custom_call_target="Cholesky" | custom-call | tf_op jit(solution)/shard_map/jit(cholesky)/cholesky | solution.py:36
  907.7 0.6 compare_reduce_fusion
  908.3 0.7 compare_reduce_fusion.2
  911.6 10.9 %while.1 = (s32[]{:T(128)}, f32[512,512]{1,0:T(8,128)S(1)}, s32[4,2]{0,1:T(2,128)S(1)}, f32[4,128,128]{2,1,0:T(8,128)}, s32[]{:T(128)}) while((s32[]{:T(128)}, f32[512,512]{1,0:T(8,128)S(1)}, s32[4,2]{0,1:T(2,128)S(1)}, f32[4,128,128]{2,1,0:T(8,128)}, s32[]{:T(128)}) %tuple.32), condition=%wide.while_cond, body=%wide.while_body.sunk | while | flops 2 | bytes 132705 | solution.py:37
  911.7 0.6 fusion.82
  912.3 2.1 bitcast_dynamic-update-slice_fusion.2
  914.5 0.6 fusion.82
  915.1 2.1 bitcast_dynamic-update-slice_fusion.2
  917.2 0.6 fusion.82
  917.8 2.1 bitcast_dynamic-update-slice_fusion.2
  919.9 0.6 fusion.82
  920.5 2.1 bitcast_dynamic-update-slice_fusion.2
  922.6 40.1 %custom-call.37 = f32[4,128,128]{1,2,0:T(8,128)S(1)} custom-call(f32[4,128,128]{2,1,0:T(8,128)} %get-tuple-element.9), custom_call_target="InvertDiagBlocksLowerTriangular" | custom-call | tf_op jit(solution)/shard_map/jit(_cho_solve)/triangular_solve | solution.py:37
  962.7 0.4 fusion.30
  963.5 0.4 fusion.51
  964.0 0.4 convolution_subtract_fusion.2
  964.4 0.4 fusion.53
  964.8 0.6 convolution_subtract_fusion.5
  965.5 0.4 fusion.55
  966.3 0.4 convolution_subtract_fusion.1
  967.1 0.5 convolution_subtract_fusion
  967.9 0.7 convolution_subtract_fusion.4
  969.0 1.9 convolution_add_fusion
  970.9 1.0 convert_bitcast_fusion
  971.9 88.4 %all-gather.9.cloned.1.call-done = bf16[4,500,512]{2,1,0:T(8,128)(2,1)} async-done(((bf16[1,500,512]{2,1,0:T(8,128)(2,1)}), bf16[4,500,512]{2,1,0:T(8,128)(2,1)}) %all-gather.9.cloned.1.call-update) | async-done | bytes 2048016 | tf_op jit(solution)/shard_map/all_gather | solution.py:43
  1060.3 1.7 reshape.88
  1062.1 5.5 add_convert_fusion
  (52 shorter events, 5.3 us)
Async XLA Ops:
  7.2 73.9 %all-gather.5.cloned.1.call-start = ((), (), s32[]{:S(2)}) async-start(), calls=%async_computation | async-start | bytes 5242880 | tf_op jit(solution)/shard_map/all_gather | solution.py:30
  7.9 138.8 %all-gather.7.cloned.1.call-start = ((), (), s32[]{:S(2)}) async-start(), calls=%async_computation.1 | async-start | bytes 5242880 | tf_op jit(solution)/shard_map/all_gather | solution.py:31
  14.2 811.9 %all-reduce.4.cloned.1.call-start = ((), (), s32[]{:S(2)}) async-start(), calls=%async_computation.3 | async-start | bytes 4194304 | tf_op jit(solution)/shard_map/psum | solution.py:34
  81.1 3.4 copy-start.1
  87.3 2.0 copy-start
  92.7 61.3 %copy-start.4 = (f32[500,512]{1,0:T(8,128)S(1)}, f32[500,512]{1,0:T(8,128)}, u32[]{:S(2)}) copy-start(f32[500,512]{1,0:T(8,128)} %param.11) | copy-start | bytes 3072004
  153.5 906.8 %all-gather.9.cloned.1.call-start = ((), (), s32[]{:S(2)}) async-start(), calls=%async_computation.2 | async-start | bytes 2580480 | tf_op jit(solution)/shard_map/all_gather | solution.py:43
  826.1 1.8 copy-start.2
  828.1 134.6 %copy-start.3 = (f32[512,512]{1,0:T(8,128)S(1)}, f32[512,512]{1,0:T(8,128)}, u32[]{:S(2)}) copy-start(f32[512,512]{1,0:T(8,128)} %get-tuple-element.18) | copy-start | bytes 3145732
  964.4 4.6 copy-start.5
  969.0 93.1 %copy-start.7 = (f32[1024]{0:T(1024)S(1)}, f32[1024]{0:T(1024)}, u32[]{:S(2)}) copy-start(f32[1024]{0:T(1024)} %param.13) | copy-start | bytes 12292
  970.9 96.6 %copy-start.6 = (f32[500,512]{1,0:T(8,128)}, f32[500,512]{1,0:T(8,128)S(1)}, u32[]{:S(2)}) copy-start(f32[500,512]{1,0:T(8,128)S(1)} %convolution_add_fusion) | copy-start | bytes 3072004
Sparse Core Ops, SparseCore 0:
  9.8 71.2 all-gather.4
  83.4 63.1 all-gather.6
  153.6 672.4 all-reduce.3
  972.0 88.2 all-gather.8
where the time goes:
time: 1080 us; the launch traced here: 1070 us
  waiting for transfers between devices  882 us (82%)
  other arithmetic  134 us (12%)
  matrix products  25.6 us (2%)
  between operations  17.1 us (2%)
  local copies, waits for them, and re-layouts  15.6 us (1%)
    psum x1, waiting for transfers between devices, shards(): gram_sum, cross = lax.psum((gram_part, cross_part), 'obs')  672 us
    all_gather x1, waiting for transfers between devices, shards(): lax.all_gather(coef_low, 'ens', axis=0, tiled=True)  88.4 us
    another operation x14, other arithmetic, shards(): factor = jnp.linalg.cholesky(gram)  78.6 us
    all_gather x1, waiting for transfers between devices, shards(): lax.all_gather(predicted, 'ens', axis=1, tiled=True)  66.9 us
    all_gather x1, waiting for transfers between devices, shards(): lax.all_gather(innovation, 'ens', axis=1, tiled=True)  53.9 us
    another operation x3, other arithmetic, shards(): weights = jax.scipy.linalg.cho_solve((factor, True), cross)  40.3 us
  transfers between devices with their start and end apart: 4, of which 4 were waited for; matrix products, arithmetic and copies ran while one was open for 1% of the time, Pallas kernels for 0%

commit v1 on v0

--- a/solution.py
+++ b/solution.py
@@ -1,9 +1,11 @@
 import jax
 import jax.numpy as jnp
 from jax import lax
+from jax.sharding import Mesh
 from jax.sharding import PartitionSpec as P
 
 ALPHA = 4
+OBS_AXES = ("y", "x", "zl")
 
 
 def member_products(gathered, innov_all, row_scale, members):
@@ -16,6 +18,24 @@
     gram_part = lax.dot_general(anomaly, anomaly, contract, preferred_element_type=jnp.float32)
     cross_part = lax.dot_general(anomaly, innov_all, contract, preferred_element_type=jnp.float32)
     return (gram_part, cross_part)
+
+
+def ring_psum(x, axes):
+    for a in axes:
+        n = lax.axis_size(a)
+        idx = lax.axis_index(a)
+        chunks = x.reshape(n, x.shape[0] // n, *x.shape[1:])
+        acc = lax.dynamic_index_in_dim(chunks, idx, 0, keepdims=False)
+        for s in range(1, n):
+            send = lax.dynamic_index_in_dim(chunks, (idx + s) % n, 0, keepdims=False)
+            acc = acc + lax.ppermute(send, a, [(i, (i + s) % n) for i in range(n)])
+        x = acc
+    for a in reversed(axes):
+        n = lax.axis_size(a)
+        idx = lax.axis_index(a)
+        parts = [x] + [lax.ppermute(x, a, [(i, (i - s) % n) for i in range(n)]) for s in range(1, n)]
+        x = jnp.roll(jnp.stack(parts), idx, axis=0).reshape(n * x.shape[0], *x.shape[1:])
+    return x
 
 
 def shards(predicted, noise, observed, obs_error, coefficients, basis, mean_field):
@@ -31,7 +51,8 @@
         lax.all_gather(innovation, "ens", axis=1, tiled=True),
     )
     gram_part, cross_part = member_products(gathered, innov_all, spread, members)
-    gram_sum, cross = lax.psum((gram_part, cross_part), "obs")
+    both = ring_psum(jnp.concatenate([gram_part, cross_part], axis=0), OBS_AXES)
+    gram_sum, cross = both[:members], both[members:]
     gram = gram_sum + jnp.eye(members, dtype=jnp.float32)
     factor = jnp.linalg.cholesky(gram)
     weights = jax.scipy.linalg.cho_solve((factor, True), cross)
@@ -50,14 +71,18 @@
 
 
 def solution(mesh):
+    obs_size, ens_size = mesh.devices.shape
+    side = round(obs_size ** (1 / 3))
+    fine = Mesh(mesh.devices.reshape(side, side, obs_size // side**2, ens_size), (*OBS_AXES, "ens"))
+    obs = OBS_AXES
     in_specs = (
-        P("obs", "ens"),
-        P("obs", "ens"),
-        P("obs"),
-        P("obs"),
+        P(obs, "ens"),
+        P(obs, "ens"),
+        P(obs),
+        P(obs),
         P("ens", None),
-        P(None, ("obs", "ens")),
-        P(("obs", "ens")),
+        P(None, (*obs, "ens")),
+        P((*obs, "ens")),
     )
-    out_specs = (P("ens", None), P(None, ("obs", "ens")))
-    return jax.shard_map(shards, mesh=mesh, in_specs=in_specs, out_specs=out_specs, check_vma=False)
+    out_specs = (P("ens", None), P(None, (*obs, "ens")))
+    return jax.shard_map(shards, mesh=fine, in_specs=in_specs, out_specs=out_specs, check_vma=False)

time: 1080 us -> 452 us (0.42)
  waiting for transfers between devices: 882 us -> 222 us
  starting transfers between devices: 0.62 us -> 24.1 us
    psum x1 -> x0, waiting for transfers between devices: 672 us -> none  [shards(): gram_sum, cross = lax.psum((gram_part, cross_part), 'obs')]
    ppermute x0 -> x18, waiting for transfers between devices: none -> 63.2 us  [the longest x9 35.3 us: ring_psum(): lax.ppermute(x, a, [(i, (i - s) % n) for i in range(n)])]
    all_gather x1, waiting for transfers between devices: 88.4 us -> 36.1 us  [shards(): lax.all_gather(coef_low, 'ens', axis=0, tiled=True)]
    ppermute x0 -> x18, starting transfers between devices: none -> 24 us  [the longest x9 13.5 us: ring_psum(): acc = acc + lax.ppermute(send, a, [(i, (i + s) % n) for i in range(n)])]
  transfers between devices with their start and end apart: 4 -> 21, of which waited for: 4 -> 19; matrix products, arithmetic and copies ran while one was open for 1% -> 4% of each run, Pallas kernels for 0% -> 0%
where the time goes in v1:
time: 452 us; the launch traced here: 443 us
  waiting for transfers between devices  222 us (49%)
  other arithmetic  136 us (30%)
  matrix products  27.2 us (6%)
  starting transfers between devices  24.1 us (5%)
  between operations  17.3 us (4%)
  local copies, waits for them, and re-layouts  16.8 us (4%)
    another operation x14, other arithmetic, shards(): factor = jnp.linalg.cholesky(gram)  78.8 us
    all_gather x1, waiting for transfers between devices, shards(): lax.all_gather(predicted, 'ens', axis=1, tiled=True)  66.8 us
    all_gather x1, waiting for transfers between devices, shards(): lax.all_gather(innovation, 'ens', axis=1, tiled=True)  55 us
    another operation x3, other arithmetic, shards(): weights = jax.scipy.linalg.cho_solve((factor, True), cross)  39.4 us
    all_gather x1, waiting for transfers between devices, shards(): lax.all_gather(coef_low, 'ens', axis=0, tiled=True)  36.1 us
    ppermute x9, waiting for transfers between devices, ring_psum(): lax.ppermute(x, a, [(i, (i - s) % n) for i in range(n)])  35.3 us
    ppermute x9, waiting for transfers between devices, ring_psum(): acc = acc + lax.ppermute(send, a, [(i, (i + s) % n) for i in range(n)])  27.9 us
    ppermute x9, starting transfers between devices, ring_psum(): acc = acc + lax.ppermute(send, a, [(i, (i + s) % n) for i in range(n)])  13.5 us
  transfers between devices with their start and end apart: 21, of which 19 were waited for; matrix products, arithmetic and copies ran while one was open for 4% of the time, Pallas kernels for 0%

profile of v1, /device:TPU:1, one launch (start us, length us, event | category | flops | bytes accessed | tf_op | source)
XLA Modules:
  0.0 442.9 jit_solution(4274285118662947647)
XLA Ops:
  8.7 5.5 %add_convert_fusion.1 = bf16[4096,128]{1,0:T(8,128)(2,1)} fusion(bf16[4096,128]{1,0:T(8,128)(2,1)} %param.8, bf16[4096,128]{1,0:T(8,128)(2,1)} %param.7, f32[4096]{0:T(1024)S(1)} %get-tuple-element.43, f32[4096]{0:T(1024)} %param.9), kind=kLoop, calls=%fused_computation.8 | loop fusion | flops 3145728 | bytes 3178496 | tf_op jit(solution)/shard_map/convert_element_type | solution.py:48
  14.3 66.8 %all-gather.5.cloned.1.call-done = bf16[4096,512]{1,0:T(8,128)(2,1)} async-done(((bf16[4096,128]{1,0:T(8,128)(2,1)}), bf16[4096,512]{1,0:T(8,128)(2,1)}) %all-gather.5.cloned.1.call-update) | async-done | bytes 4194320 | tf_op jit(solution)/shard_map/all_gather | solution.py:50
  81.1 3.0 convert_reduce_fusion
  84.5 2.8 fusion.1
  87.3 2.0 copy-done
  89.3 2.4 fusion.73
  91.6 55.0 %all-gather.7.cloned.1.call-done = bf16[4096,512]{1,0:T(8,128)(2,1)} async-done(((bf16[4096,128]{1,0:T(8,128)(2,1)}), bf16[4096,512]{1,0:T(8,128)(2,1)}) %all-gather.7.cloned.1.call-update) | async-done | bytes 4194320 | tf_op jit(solution)/shard_map/all_gather | solution.py:51
  146.7 5.8 %fusion.74 = f32[512,512]{1,0:T(8,128)S(1)} fusion(bf16[4096,512]{1,0:T(8,128)(2,1)} %copy-done, bf16[4096,512]{1,0:T(8,128)(2,1)} %all-gather.7.cloned.1.call-done), kind=kOutput, calls=%fused_computation.164 | convolution fusion | flops 2147483648 | bytes 9437184 | tf_op jit(solution)/shard_map/dot_general | solution.py:19
  154.8 2.4 collective-permute-start.1
  158.4 9.9 %collective-permute-done = f32[256,512]{1,0:T(8,128)} collective-permute-done((f32[256,512]{1,0:T(8,128)}, f32[256,512]{1,0:T(8,128)}, u32[]{:S(2)}, u32[]{:S(2)}) %collective-permute-start) | collective-permute-done | bytes 524320 | tf_op jit(solution)/shard_map/ppermute | solution.py:31
  168.4 12.2 %collective-permute-done.1 = f32[256,512]{1,0:T(8,128)} collective-permute-done((f32[256,512]{1,0:T(8,128)S(1)}, f32[256,512]{1,0:T(8,128)}, u32[]{:S(2)}, u32[]{:S(2)}) %collective-permute-start.1) | collective-permute-done | bytes 524320 | tf_op jit(solution)/shard_map/ppermute | solution.py:31
  180.6 1.6 fusion.31
  182.2 1.3 collective-permute-start.3
  183.4 2.4 collective-permute-start.4
  187.3 3.6 collective-permute-done.4
  192.1 3.2 collective-permute-start.8
  196.8 3.1 collective-permute-start.9
  200.9 2.7 collective-permute-done.10
  204.7 3.3 collective-permute-start.12
  208.7 2.6 collective-permute-done.12
  211.3 2.1 collective-permute-done.13
  213.4 1.3 collective-permute-done.14
  214.8 2.1 collective-permute-start.15
  217.0 1.4 reduce_sum.18
  219.2 5.3 %collective-permute-done.15 = f32[256,512]{1,0:T(8,128)S(1)} collective-permute-done((f32[256,512]{1,0:T(8,128)S(1)}, f32[256,512]{1,0:T(8,128)S(1)}, u32[]{:S(2)}, u32[]{:S(2)}) %collective-permute-start.15) | collective-permute-done | bytes 524320 | tf_op jit(solution)/shard_map/ppermute | solution.py:36
  224.5 3.5 collective-permute-done.16
  228.1 16.2 %collective-permute-done.17 = f32[256,512]{1,0:T(8,128)S(1)} collective-permute-done((f32[256,512]{1,0:T(8,128)S(1)}, f32[256,512]{1,0:T(8,128)S(1)}, u32[]{:S(2)}, u32[]{:S(2)}) %collective-permute-start.17) | collective-permute-done | bytes 524320 | tf_op jit(solution)/shard_map/ppermute | solution.py:36
  246.2 1.6 copy.27
  248.9 11.7 %cholesky.104 = f32[128,128]{1,0:T(8,128)S(1)} custom-call(f32[128,128]{1,0:T(8,128)S(1)} %cholesky.266), custom_call_target="Cholesky" | custom-call | tf_op jit(solution)/shard_map/jit(cholesky)/cholesky | solution.py:57
  260.8 9.8 %custom-call.34 = f32[1,128,128]{1,2,0:T(8,128)S(1)} custom-call(f32[1,128,128]{2,1,0:T(8,128)S(1)} %get-tuple-element.42), custom_call_target="InvertDiagBlocksLowerTriangular" | custom-call | tf_op jit(solution)/shard_map/jit(cholesky)/cholesky | solution.py:57
  270.6 1.2 constant_dynamic-update-slice_fusion.8
  271.9 1.3 convolution_subtract_fusion.3
  273.1 11.7 %cholesky.217 = f32[128,128]{1,0:T(8,128)S(1)} custom-call(f32[128,128]{1,0:T(8,128)S(1)} %cholesky.270), custom_call_target="Cholesky" | custom-call | tf_op jit(solution)/shard_map/jit(cholesky)/cholesky | solution.py:57
  284.9 10.0 %custom-call.35 = f32[1,128,128]{1,2,0:T(8,128)S(1)} custom-call(f32[1,128,128]{2,1,0:T(8,128)S(1)} %get-tuple-element.39), custom_call_target="InvertDiagBlocksLowerTriangular" | custom-call | tf_op jit(solution)/shard_map/jit(cholesky)/cholesky | solution.py:57
  295.2 1.3 convolution_subtract_fusion.4
  296.5 11.7 %cholesky.238 = f32[128,128]{1,0:T(8,128)S(1)} custom-call(f32[128,128]{1,0:T(8,128)S(1)} %cholesky.275), custom_call_target="Cholesky" | custom-call | tf_op jit(solution)/shard_map/jit(cholesky)/cholesky | solution.py:57
  308.8 9.8 %custom-call.36 = f32[1,128,128]{1,2,0:T(8,128)S(1)} custom-call(f32[1,128,128]{2,1,0:T(8,128)S(1)} %get-tuple-element.36), custom_call_target="InvertDiagBlocksLowerTriangular" | custom-call | tf_op jit(solution)/shard_map/jit(cholesky)/cholesky | solution.py:57
  320.1 11.9 %cholesky.255 = f32[128,128]{1,0:T(8,128)S(1)} custom-call(f32[128,128]{1,0:T(8,128)S(1)} %convolution_subtract_fusion.5), custom_call_target="Cholesky" | custom-call | tf_op jit(solution)/shard_map/jit(cholesky)/cholesky | solution.py:57
  336.1 8.0 %while.1 = (s32[]{:T(128)}, f32[512,512]{1,0:T(8,128)S(1)}, s32[4,2]{0,1:T(2,128)S(1)}, f32[4,128,128]{2,1,0:T(8,128)S(1)}, s32[]{:T(128)}) while((s32[]{:T(128)}, f32[512,512]{1,0:T(8,128)S(1)}, s32[4,2]{0,1:T(2,128)S(1)}, f32[4,128,128]{2,1,0:T(8,128)S(1)}, s32[]{:T(128)}) %tuple.40), condition=%wide.while_cond, body=%wide.while_body.sunk | while | flops 2 | bytes 131181 | solution.py:58
  336.7 1.4 bitcast_dynamic-update-slice_fusion.18
  338.7 1.4 bitcast_dynamic-update-slice_fusion.18
  340.7 1.4 bitcast_dynamic-update-slice_fusion.18
  342.7 1.4 bitcast_dynamic-update-slice_fusion.18
  344.1 39.3 %custom-call.37 = f32[4,128,128]{1,2,0:T(8,128)S(1)} custom-call(f32[4,128,128]{2,1,0:T(8,128)S(1)} %get-tuple-element.9), custom_call_target="InvertDiagBlocksLowerTriangular" | custom-call | tf_op jit(solution)/shard_map/jit(_cho_solve)/triangular_solve | solution.py:58
  389.7 1.9 convolution_add_fusion
  392.6 36.1 %all-gather.9.cloned.1.call-done = bf16[4,500,512]{2,1,0:T(8,128)(2,1)} async-done(((bf16[1,500,512]{2,1,0:T(8,128)(2,1)}), bf16[4,500,512]{2,1,0:T(8,128)(2,1)}) %all-gather.9.cloned.1.call-update) | async-done | bytes 2048016 | tf_op jit(solution)/shard_map/all_gather | solution.py:64
  428.7 1.7 reshape.111
  430.5 5.5 %add_convert_fusion = bf16[512,1024]{1,0:T(8,128)(2,1)} fusion(bf16[2000,512]{1,0:T(8,128)(2,1)S(1)} %reshape.111, bf16[2000,1024]{1,0:T(8,128)(2,1)} %param.12, f32[1024]{0:T(1024)S(1)} %copy-done.5), kind=kOutput, calls=%fused_computation.7 | convolution fusion | flops 2098200576 | bytes 7196672 | tf_op jit(solution)/shard_map/dot_general | solution.py:63
  (115 shorter events, 30.1 us)
Async XLA Ops:
  7.2 73.9 %all-gather.5.cloned.1.call-start = ((), (), s32[]{:S(2)}) async-start(), calls=%async_computation | async-start | bytes 5242880 | tf_op jit(solution)/shard_map/all_gather | solution.py:50
  7.9 138.8 %all-gather.7.cloned.1.call-start = ((), (), s32[]{:S(2)}) async-start(), calls=%async_computation.1 | async-start | bytes 5242880 | tf_op jit(solution)/shard_map/all_gather | solution.py:51
  14.2 414.5 %all-gather.9.cloned.1.call-start = ((), (), s32[]{:S(2)}) async-start(), calls=%async_computation.2 | async-start | bytes 2580480 | tf_op jit(solution)/shard_map/all_gather | solution.py:64
  81.1 3.4 copy-start.1
  87.3 2.0 copy-start
  153.6 14.8 %collective-permute-start = (f32[256,512]{1,0:T(8,128)}, f32[256,512]{1,0:T(8,128)}, u32[]{:S(2)}, u32[]{:S(2)}) collective-permute-start(f32[256,512]{1,0:T(8,128)} %get-tuple-element.24), channel_id=1, source_target_pairs={{0,64},{64,128},{128,192},{192,0},{1,65},{65,129},{129,193},{193,1... | collective-permute-start | bytes 1572872 | tf_op jit(solution)/shard_map/ppermute | solution.py:31
  154.8 25.7 %collective-permute-start.1 = (f32[256,512]{1,0:T(8,128)S(1)}, f32[256,512]{1,0:T(8,128)}, u32[]{:S(2)}, u32[]{:S(2)}) collective-permute-start(f32[256,512]{1,0:T(8,128)S(1)} %get-tuple-element.26), channel_id=1, source_target_pairs={{0,128},{64,192},{128,0},{192,64},{1,129},{65,193},{129,1},{193,65... | collective-permute-start | bytes 1572872 | tf_op jit(solution)/shard_map/ppermute | solution.py:31
  157.2 23.3 %collective-permute-start.2 = (f32[256,512]{1,0:T(8,128)S(1)}, f32[256,512]{1,0:T(8,128)}, u32[]{:S(2)}, u32[]{:S(2)}) collective-permute-start(f32[256,512]{1,0:T(8,128)S(1)} %get-tuple-element.25), channel_id=1, source_target_pairs={{0,192},{64,0},{128,64},{192,128},{1,193},{65,1},{129,65},{193,129... | collective-permute-start | bytes 1572872 | tf_op jit(solution)/shard_map/ppermute | solution.py:31
  182.2 5.1 %collective-permute-start.3 = (f32[64,512]{1,0:T(8,128)S(1)}, f32[64,512]{1,0:T(8,128)S(1)}, u32[]{:S(2)}, u32[]{:S(2)}) collective-permute-start(f32[64,512]{1,0:T(8,128)S(1)} %get-tuple-element.27), channel_id=1, source_target_pairs={{0,16},{16,32},{32,48},{48,0},{1,17},{17,33},{33,49},{49,1},{2,18}... | collective-permute-start | bytes 393224 | tf_op jit(solution)/shard_map/ppermute | solution.py:31
  183.4 7.4 %collective-permute-start.4 = (f32[64,512]{1,0:T(8,128)S(1)}, f32[64,512]{1,0:T(8,128)S(1)}, u32[]{:S(2)}, u32[]{:S(2)}) collective-permute-start(f32[64,512]{1,0:T(8,128)S(1)} %get-tuple-element.29), channel_id=1, source_target_pairs={{0,32},{16,48},{32,0},{48,16},{1,33},{17,49},{33,1},{49,17},{2,34}... | collective-permute-start | bytes 393224 | tf_op jit(solution)/shard_map/ppermute | solution.py:31
  185.8 5.5 %collective-permute-start.5 = (f32[64,512]{1,0:T(8,128)S(1)}, f32[64,512]{1,0:T(8,128)S(1)}, u32[]{:S(2)}, u32[]{:S(2)}) collective-permute-start(f32[64,512]{1,0:T(8,128)S(1)} %get-tuple-element.28), channel_id=1, source_target_pairs={{0,48},{16,0},{32,16},{48,32},{1,49},{17,1},{33,17},{49,33},{2,50}... | collective-permute-start | bytes 393224 | tf_op jit(solution)/shard_map/ppermute | solution.py:31
  191.4 4.7 %collective-permute-start.6 = (f32[16,512]{1,0:T(8,128)S(1)}, f32[16,512]{1,0:T(8,128)S(1)}, u32[]{:S(2)}, u32[]{:S(2)}) collective-permute-start(f32[16,512]{1,0:T(8,128)S(1)} %get-tuple-element.30), channel_id=1, source_target_pairs={{0,4},{4,8},{8,12},{12,0},{1,5},{5,9},{9,13},{13,1},{2,6},{6,10},{... | collective-permute-start | bytes 98312 | tf_op jit(solution)/shard_map/ppermute | solution.py:31
  191.6 4.5 %collective-permute-start.7 = (f32[16,512]{1,0:T(8,128)S(1)}, f32[16,512]{1,0:T(8,128)S(1)}, u32[]{:S(2)}, u32[]{:S(2)}) collective-permute-start(f32[16,512]{1,0:T(8,128)S(1)} %get-tuple-element.32), channel_id=1, source_target_pairs={{0,8},{4,12},{8,0},{12,4},{1,9},{5,13},{9,1},{13,5},{2,10},{6,14},... | collective-permute-start | bytes 98312 | tf_op jit(solution)/shard_map/ppermute | solution.py:31
  192.1 4.7 %collective-permute-start.8 = (f32[16,512]{1,0:T(8,128)S(1)}, f32[16,512]{1,0:T(8,128)S(1)}, u32[]{:S(2)}, u32[]{:S(2)}) collective-permute-start(f32[16,512]{1,0:T(8,128)S(1)} %get-tuple-element.31), channel_id=1, source_target_pairs={{0,12},{4,0},{8,4},{12,8},{1,13},{5,1},{9,5},{13,9},{2,14},{6,2},{... | collective-permute-start | bytes 98312 | tf_op jit(solution)/shard_map/ppermute | solution.py:31
  196.8 4.2 collective-permute-start.9
  199.9 3.7 collective-permute-start.10
  199.9 4.7 %collective-permute-start.11 = (f32[16,512]{1,0:T(8,128)S(1)}, f32[16,512]{1,0:T(8,128)S(1)}, u32[]{:S(2)}, u32[]{:S(2)}) collective-permute-start(f32[16,512]{1,0:T(8,128)S(1)} %get-tuple-element.19), channel_id=1, source_target_pairs={{0,4},{4,8},{8,12},{12,0},{1,5},{5,9},{9,13},{13,1},{2,6},{6,10},{... | collective-permute-start | bytes 98312 | tf_op jit(solution)/shard_map/ppermute | solution.py:36
  204.7 6.6 %collective-permute-start.12 = (f32[64,512]{1,0:T(8,128)S(1)}, f32[64,512]{1,0:T(8,128)S(1)}, u32[]{:S(2)}, u32[]{:S(2)}) collective-permute-start(f32[64,512]{1,0:T(8,128)S(1)} %bitcast.160), channel_id=1, source_target_pairs={{0,48},{16,0},{32,16},{48,32},{1,49},{17,1},{33,17},{49,33},{2,50}... | collective-permute-start | bytes 393224 | tf_op jit(solution)/shard_map/ppermute | solution.py:36
  208.0 5.4 %collective-permute-start.13 = (f32[64,512]{1,0:T(8,128)S(1)}, f32[64,512]{1,0:T(8,128)S(1)}, u32[]{:S(2)}, u32[]{:S(2)}) collective-permute-start(f32[64,512]{1,0:T(8,128)S(1)} %bitcast.161), channel_id=1, source_target_pairs={{0,32},{16,48},{32,0},{48,16},{1,33},{17,49},{33,1},{49,17},{2,34}... | collective-permute-start | bytes 393224 | tf_op jit(solution)/shard_map/ppermute | solution.py:36
  208.4 6.3 %collective-permute-start.14 = (f32[64,512]{1,0:T(8,128)S(1)}, f32[64,512]{1,0:T(8,128)S(1)}, u32[]{:S(2)}, u32[]{:S(2)}) collective-permute-start(f32[64,512]{1,0:T(8,128)S(1)} %bitcast.162), channel_id=1, source_target_pairs={{0,16},{16,32},{32,48},{48,0},{1,17},{17,33},{33,49},{49,1},{2,18}... | collective-permute-start | bytes 393224 | tf_op jit(solution)/shard_map/ppermute | solution.py:36
  214.8 9.7 %collective-permute-start.15 = (f32[256,512]{1,0:T(8,128)S(1)}, f32[256,512]{1,0:T(8,128)S(1)}, u32[]{:S(2)}, u32[]{:S(2)}) collective-permute-start(f32[256,512]{1,0:T(8,128)S(1)} %bitcast.148), channel_id=1, source_target_pairs={{0,192},{64,0},{128,64},{192,128},{1,193},{65,1},{129,65},{193,129... | collective-permute-start | bytes 1572872 | tf_op jit(solution)/shard_map/ppermute | solution.py:36
  218.3 9.7 %collective-permute-start.16 = (f32[256,512]{1,0:T(8,128)S(1)}, f32[256,512]{1,0:T(8,128)S(1)}, u32[]{:S(2)}, u32[]{:S(2)}) collective-permute-start(f32[256,512]{1,0:T(8,128)S(1)} %bitcast.149), channel_id=1, source_target_pairs={{0,128},{64,192},{128,0},{192,64},{1,129},{65,193},{129,1},{193,65... | collective-permute-start | bytes 1572872 | tf_op jit(solution)/shard_map/ppermute | solution.py:36
  218.9 25.4 %collective-permute-start.17 = (f32[256,512]{1,0:T(8,128)S(1)}, f32[256,512]{1,0:T(8,128)S(1)}, u32[]{:S(2)}, u32[]{:S(2)}) collective-permute-start(f32[256,512]{1,0:T(8,128)S(1)} %bitcast.150), channel_id=1, source_target_pairs={{0,64},{64,128},{128,192},{192,0},{1,65},{65,129},{129,193},{193,1... | collective-permute-start | bytes 1572872 | tf_op jit(solution)/shard_map/ppermute | solution.py:36
  247.9 1.0 copy-start.2
  385.5 4.2 copy-start.3
  389.7 40.8 %copy-start.5 = (f32[1024]{0:T(1024)S(1)}, f32[1024]{0:T(1024)}, u32[]{:S(2)}) copy-start(f32[1024]{0:T(1024)} %param.13) | copy-start | bytes 12292
  391.6 44.3 %copy-start.4 = (f32[500,512]{1,0:T(8,128)}, f32[500,512]{1,0:T(8,128)S(1)}, u32[]{:S(2)}) copy-start(f32[500,512]{1,0:T(8,128)S(1)} %convolution_add_fusion) | copy-start | bytes 3072004
Sparse Core Ops, SparseCore 0:
  9.8 71.2 all-gather.4
  83.4 63.1 all-gather.6
  392.7 35.9 all-gather.8
